TPU v7x, 256 devices: a whole 4x4x8 slice. The times are simulated.
256 devices in a mesh: ctx: 32 (over z, x), head: 8 (over y, core).
Axes of the slice: x: 4, y: 4, z: 8, core: 2. Of those that a mesh axis runs over, the one named last changes fastest.
Arguments:
- query_matrix: bfloat16 [32768, 4096], P(('ctx', 'head')), may hold values from -5 to 5
- key_matrix: bfloat16 [32768, 1024], P(('ctx', 'head')), may hold values from -5 to 5
- value_matrix: bfloat16 [32768, 1024], P(('ctx', 'head')), may hold values from -12 to 12
- output_gradient: bfloat16 [32768, 4096], P('ctx', 'head'), may hold values from -12 to 12
- doc_start: int32 [128], replicated, may hold values from 0 to 1, as said below
Outputs:
- attended: bfloat16 [32768, 4096], P('ctx', 'head')
- grad_q: bfloat16 [32768, 4096], P('ctx', 'head')
- grad_k: bfloat16 [32768, 1024], P('ctx', 'head')
- grad_v: bfloat16 [32768, 1024], P('ctx', 'head')
Inputs may be any that keep to these rules, and one draw needn't show every extreme that they name: `doc_start`: entry 0 is 1; a document starts at each unit whose entry is 1 and lasts to the next start or the end; every document has 1 to 4 units, and some document has exactly 1024 tokens.
All inputs are finite; a program needn't handle non-finite values.
Results may differ from a plain program's by a relative error of at most 0.019.
Values may be sent and summed in bfloat16 or wider, within the bound.
No kernel may reach another device: no remote copies, remote signals or barrier semaphores. Data moves between devices by JAX's collectives and lax.ppermute only.
A program may use at most 64 MiB of HBM per device.

v0:
```python
import jax
import jax.numpy as jnp
from jax import lax
from jax.sharding import PartitionSpec as P

QUERY_HEADS = 32
KEY_VALUE_HEADS = 8
HEAD_SIZE = 128


def from_behind(block, axis, distance):
    devices = range(lax.axis_size(axis))
    route = [(i - distance, i) for i in devices if i - distance in devices]
    return lax.ppermute(block, axis, route)


def tile_grads(query_tile, grad_tile, key_rows, value_rows, query_doc, key_doc, query_pos, key_pos):
    score_scale = query_tile.shape[-1] ** (-0.5)
    scores = (
        jnp.einsum("tgrd,ngd->grtn", query_tile, key_rows, preferred_element_type=jnp.float32)
        * score_scale
    )
    visible = (key_doc[None, :] == query_doc[:, None]) & (key_pos[None, :] <= query_pos[:, None])
    scores = jnp.where(visible, scores, -jnp.inf)
    row_top = jnp.max(scores, axis=-1, keepdims=True)
    log_total = row_top + jnp.log(jnp.sum(jnp.exp(scores - row_top), axis=-1, keepdims=True))
    weights = jnp.exp(scores - log_total)
    weights_low = weights.astype(jnp.bfloat16)
    attended = jnp.einsum(
        "grtn,ngd->tgrd", weights_low, value_rows, preferred_element_type=jnp.float32
    ).astype(jnp.bfloat16)
    row_delta = jnp.sum(grad_tile.astype(jnp.float32) * attended.astype(jnp.float32), axis=-1)
    row_delta = jnp.transpose(row_delta, (1, 2, 0))[..., None]
    grad_weights = jnp.einsum(
        "tgrd,ngd->grtn", grad_tile, value_rows, preferred_element_type=jnp.float32
    )
    grad_scores = (weights * (grad_weights - row_delta)).astype(jnp.bfloat16)
    grad_query = (
        jnp.einsum("grtn,ngd->tgrd", grad_scores, key_rows, preferred_element_type=jnp.float32)
        * score_scale
    ).astype(jnp.bfloat16)
    grad_key = (
        jnp.einsum("grtn,tgrd->ngd", grad_scores, query_tile, preferred_element_type=jnp.float32)
        * score_scale
    )
    grad_value = jnp.einsum(
        "grtn,tgrd->ngd", weights_low, grad_tile, preferred_element_type=jnp.float32
    )
    return (attended, grad_query, grad_key, grad_value)


def local(query_matrix, key_matrix, value_matrix, output_gradient, doc_start):
    token_per_shard = query_matrix.shape[0]
    head_groups = lax.axis_size("head")
    q_cols = query_matrix.shape[1] // head_groups
    k_cols = key_matrix.shape[1] // head_groups
    packed = jnp.concatenate(
        [
            query_matrix.reshape(token_per_shard, head_groups, q_cols),
            key_matrix.reshape(token_per_shard, head_groups, k_cols),
            value_matrix.reshape(token_per_shard, head_groups, k_cols),
        ],
        axis=2,
    )
    packed = lax.all_to_all(packed, "head", split_axis=1, concat_axis=0, tiled=True)
    ctx_rows = packed.shape[0]
    packed = packed.reshape(ctx_rows, q_cols + 2 * k_cols)
    kv_local = k_cols // HEAD_SIZE
    heads_per_group = q_cols // k_cols
    query_array = packed[:, :q_cols].reshape(ctx_rows, kv_local, heads_per_group, HEAD_SIZE)
    own_kv = packed[:, q_cols:]
    own_keys = own_kv[:, :k_cols].reshape(ctx_rows, kv_local, HEAD_SIZE)
    own_values = own_kv[:, k_cols:].reshape(ctx_rows, kv_local, HEAD_SIZE)
    unit_rows = 2 * token_per_shard
    earlier_kv = from_behind(own_kv, "ctx", 1)
    earlier_keys = earlier_kv[:, :k_cols].reshape(ctx_rows, kv_local, HEAD_SIZE)
    earlier_values = earlier_kv[:, k_cols:].reshape(ctx_rows, kv_local, HEAD_SIZE)
    gradient_per_head = output_gradient.reshape(ctx_rows, kv_local, heads_per_group, HEAD_SIZE)
    per_shard = ctx_rows // unit_rows
    ctx_index = lax.axis_index("ctx")
    unit_doc = jnp.cumsum(doc_start)
    own_units = lax.dynamic_slice_in_dim(unit_doc, ctx_index * per_shard, per_shard)
    prior_units = lax.dynamic_slice_in_dim(
        unit_doc, jnp.maximum(ctx_index - 1, 0) * per_shard, per_shard
    )
    prior_units = jnp.where(ctx_index > 0, prior_units, -1)
    own_doc = jnp.repeat(own_units, unit_rows, total_repeat_length=ctx_rows)
    prior_doc = jnp.repeat(prior_units, unit_rows, total_repeat_length=ctx_rows)
    joined_keys = jnp.concatenate([earlier_keys, own_keys], axis=0)
    joined_values = jnp.concatenate([earlier_values, own_values], axis=0)
    joined_doc = jnp.concatenate([prior_doc, own_doc], axis=0)
    joined_pos = jnp.arange(ctx_rows + ctx_rows, dtype=jnp.int32) - ctx_rows
    before = ctx_rows - unit_rows
    key_grad = jnp.zeros((ctx_rows + ctx_rows, kv_local, HEAD_SIZE), jnp.float32)
    value_grad = jnp.zeros((ctx_rows + ctx_rows, kv_local, HEAD_SIZE), jnp.float32)
    pieces = []
    query_grads = []
    for unit_number in range(per_shard):
        first_row = unit_number * unit_rows
        end_row = first_row + unit_rows
        window_start = ctx_rows - before + first_row
        window_end = window_start + ctx_rows
        query_tile = query_array[first_row:end_row]
        grad_tile = gradient_per_head[first_row:end_row]
        query_doc = own_doc[first_row:end_row]
        query_pos = jnp.arange(first_row, end_row, dtype=jnp.int32)
        results = tile_grads(
            query_tile,
            grad_tile,
            joined_keys[window_start:window_end],
            joined_values[window_start:window_end],
            query_doc,
            joined_doc[window_start:window_end],
            query_pos,
            joined_pos[window_start:window_end],
        )
        attended, grad_query, grad_key, grad_value = results
        pieces.append(attended)
        query_grads.append(grad_query)
        key_grad = key_grad.at[window_start:window_end].add(grad_key)
        value_grad = value_grad.at[window_start:window_end].add(grad_value)
    prior_grads = jnp.concatenate(
        [
            key_grad[:ctx_rows].astype(jnp.bfloat16).reshape(ctx_rows, k_cols),
            value_grad[:ctx_rows].astype(jnp.bfloat16).reshape(ctx_rows, k_cols),
        ],
        axis=1,
    )
    later = from_behind(prior_grads, "ctx", -1).astype(jnp.float32)
    key_own = key_grad[ctx_rows:].reshape(ctx_rows, k_cols) + later[:, :k_cols]
    value_own = value_grad[ctx_rows:].reshape(ctx_rows, k_cols) + later[:, k_cols:]
    summed_keys = key_own.astype(jnp.bfloat16)
    summed_values = value_own.astype(jnp.bfloat16)
    attended_all = jnp.concatenate(pieces, axis=0).reshape(
        ctx_rows, kv_local * heads_per_group * HEAD_SIZE
    )
    query_total = jnp.concatenate(query_grads, axis=0).reshape(
        ctx_rows, kv_local * heads_per_group * HEAD_SIZE
    )
    return (attended_all, query_total, summed_keys, summed_values)


def solution(mesh):
    placed = (
        P(("ctx", "head"), None),
        P(("ctx", "head"), None),
        P(("ctx", "head"), None),
        P("ctx", "head"),
        P(),
    )
    return jax.shard_map(
        local,
        mesh=mesh,
        in_specs=placed,
        out_specs=(P("ctx", "head"), P("ctx", "head"), P("ctx", "head"), P("ctx", "head")),
        check_vma=False,
    )
```

profile of v0, /device:TPU:102, one launch (start us, length us, event | category | flops | bytes accessed | tf_op | source)
XLA Modules:
  0.0 101.2 jit_solution(3459865520196995552)
XLA Ops:
  0.6 1.4 %copy.156 = bf16[16,8,8,512]{3,2,0,1:T(8,128)(2,1)S(1)} copy(bf16[16,8,8,512]{3,2,1,0:T(8,128)(2,1)} %bitcast.542) | data formatting | bytes 2097152 | tf_op jit(solution)/shard_map/reshape | solution.py:59
  4.5 4.5 %all-to-all-start = ((bf16[128,8,768]{2,0,1:T(8,128)(2,1)}), bf16[128,8,768]{2,0,1:T(8,128)(2,1)S(1)}, u32[]{:S(2)}, u32[]{:S(2)}) async-start(bf16[128,8,768]{2,0,1:T(8,128)(2,1)} %pad_maximum_fusion), calls=%async_computation | async-start | bytes 3145728 | tf_op jit(solution)/shard_map/all_to_all | solution.py:65
  11.1 5.0 %select_select_fusion.1 = (s32[1024]{0:T(1024)S(1)}, s32[1024]{0:T(1024)S(1)}) fusion(pred[1024]{0:T(1024)(128)(4,1)S(1)} %copy-done.12, pred[1024]{0:T(1024)(128)(4,1)S(1)} %copy-done.13, pred[1024]{0:T(1024)(128)(4,1)S(1)} %copy-done.14, s32[]{:T(128)} %bitcast.13, s32[]{:T(128)} %bitcast.12, s32[]{:T(128)} %bitcast.11, s32[]{:T(128)} %bitcast.10, ...), kind=kLoop, calls=%fused_computation.171 | loop fusion | flops 6144 | bytes 11296 | tf_op jit(solution)/shard_map/jit(_take)/gather | solution.py:88
  16.1 1.8 %copy.143 = bf16[256,512]{0,1:T(8,128)(2,1)} copy(bf16[256,512]{1,0:T(8,128)(2,1)} %get-tuple-element.137) | data formatting | bytes 524288
  17.9 1.8 %copy.144 = bf16[256,512]{0,1:T(8,128)(2,1)} copy(bf16[256,512]{1,0:T(8,128)(2,1)} %get-tuple-element.139) | data formatting | bytes 524288
  22.8 7.7 %all-to-all-done = bf16[128,8,768]{2,0,1:T(8,128)(2,1)S(1)} async-done(((bf16[128,8,768]{2,0,1:T(8,128)(2,1)}), bf16[128,8,768]{2,0,1:T(8,128)(2,1)S(1)}, u32[]{:S(2)}, u32[]{:S(2)}) %all-to-all-start) | async-done | bytes 1572896 | tf_op jit(solution)/shard_map/all_to_all | solution.py:65
  32.3 5.1 %collective-permute-start = (bf16[1024,256]{1,0:T(8,128)(2,1)}, bf16[1024,256]{1,0:T(8,128)(2,1)}, u32[]{:S(2)}, u32[]{:S(2)}) collective-permute-start(bf16[1024,256]{1,0:T(8,128)(2,1)} %slice.388), channel_id=1, source_target_pairs={{0,8},{8,16},{16,24},{24,32},{32,40},{40,48},{48,56},{56,64},{64,7... | collective-permute-start | bytes 1572872 | tf_op jit(solution)/shard_map/ppermute | solution.py:14
  40.2 1.9 %fusion.141 = (f32[256,4]{0,1:T(4,128)S(1)}, bf16[256,1,4,128]{0,3,2,1:T(8,128)(2,1)}) fusion(bf16[256,1,4,128]{0,3,2,1:T(8,128)(2,1)S(1)} %bitcast.547, f32[1024,256,4]{1,0,2:T(8,128)S(1)} %get-tuple-element.165, f32[4,256]{1,0:T(4,128)S(1)} %log_add_fusion, pred[256,1024]{0,1:T(8,128)(4,1)S(1)} %compare_and_fusion, bf16[1024,768]{1,0:T(8,128)(2,1)S(1)} %bitcast.531), kind=kOutput, calls=%fused_computation.125 | convolution fusion | flops 273284096 | bytes 5251072 | tf_op jit(solution)/shard_map/grtn,ngd->tgrd/dot_general | solution.py:29
  42.2 2.7 %fusion.1 = bf16[1,4,256,1024]{2,3,1,0:T(8,128)(2,1)} fusion(f32[1024,256,4]{1,0,2:T(8,128)S(1)} %get-tuple-element.165, bf16[256,4,128]{0,2,1:T(8,128)(2,1)S(1)} %bitcast.548, f32[4,256]{1,0:T(4,128)S(1)} %bitcast.562, f32[4,256]{1,0:T(4,128)S(1)} %log_add_fusion, pred[256,1024]{0,1:T(8,128)(4,1)S(1)} %compare_and_fusion, bf16[1024,768]{1,0:T(8,128)(2,1)S(1)} %bitcast.532), kind=kOutput, calls=%fused_computation.2 | convolution fusion | flops 274726912 | bytes 7086080 | tf_op jit(solution)/shard_map/tgrd,ngd->grtn/dot_general | solution.py:34
  44.8 1.8 %copy.59 = bf16[256,512]{0,1:T(8,128)(2,1)} copy(bf16[256,512]{1,0:T(8,128)(2,1)} %get-tuple-element.131) | data formatting | bytes 524288 | tf_op jit(solution)/shard_map/slice | solution.py:103
  48.5 2.1 %fusion.129 = bf16[256,1,4,128]{0,3,2,1:T(8,128)(2,1)S(1)} fusion(bf16[1,4,256,1024]{2,3,1,0:T(8,128)(2,1)} %fusion.1, bf16[1024,768]{1,0:T(8,128)(2,1)S(1)} %bitcast.533), kind=kOutput, calls=%fused_computation.96 | convolution fusion | flops 268697600 | bytes 2621440 | tf_op jit(solution)/shard_map/grtn,ngd->tgrd/dot_general | solution.py:39
  54.8 1.9 %fusion.144 = (f32[256,4]{0,1:T(4,128)S(1)}, bf16[256,1,4,128]{0,3,2,1:T(8,128)(2,1)}) fusion(bf16[256,1,4,128]{0,3,2,1:T(8,128)(2,1)S(1)} %bitcast.557, f32[1024,256,4]{1,0,2:T(8,128)S(1)} %get-tuple-element.171, f32[4,256]{1,0:T(4,128)S(1)} %log_add_fusion.3, pred[256,1024]{0,1:T(8,128)(4,1)S(1)} %fusion.136, ...), kind=kOutput, calls=%fused_computation.131 | convolution fusion | flops 273808384 | bytes 5513216 | tf_op jit(solution)/shard_map/grtn,ngd->tgrd/dot_general | solution.py:29
  56.7 1.3 %fusion.7 = bf16[1,4,256,1024]{2,3,1,0:T(8,128)(2,1)S(1)} fusion(f32[1024,256,4]{1,0,2:T(8,128)S(1)} %get-tuple-element.171, bf16[256,4,128]{0,2,1:T(8,128)(2,1)S(1)} %bitcast.558, f32[4,256]{1,0:T(4,128)S(1)} %bitcast.560, f32[4,256]{1,0:T(4,128)S(1)} %log_add_fusion.3, pred[256,1024]{0,1:T(8,128)(4,1)S(1)} %fusion.136, ...), kind=kOutput, calls=%fused_computation.11 | convolution fusion | flops 275251200 | bytes 7348224 | tf_op jit(solution)/shard_map/tgrd,ngd->grtn/dot_general | solution.py:34
  63.2 1.9 %fusion.143 = (f32[256,4]{0,1:T(4,128)S(1)}, bf16[256,1,4,128]{0,3,2,1:T(8,128)(2,1)}) fusion(bf16[256,1,4,128]{0,3,2,1:T(8,128)(2,1)S(1)} %bitcast.553, f32[1024,256,4]{1,0,2:T(8,128)S(1)} %get-tuple-element.169, f32[4,256]{1,0:T(4,128)S(1)} %log_add_fusion.2, pred[256,1024]{0,1:T(8,128)(4,1)S(1)} %compare_and_fusion.2, ...), kind=kOutput, calls=%fused_computation.129 | convolution fusion | flops 273808384 | bytes 5513216 | tf_op jit(solution)/shard_map/grtn,ngd->tgrd/dot_general | solution.py:29
  65.1 1.3 %fusion.5 = bf16[1,4,256,1024]{2,3,1,0:T(8,128)(2,1)S(1)} fusion(f32[1024,256,4]{1,0,2:T(8,128)S(1)} %get-tuple-element.169, bf16[256,4,128]{0,2,1:T(8,128)(2,1)S(1)} %bitcast.554, f32[4,256]{1,0:T(4,128)S(1)} %bitcast.563, f32[4,256]{1,0:T(4,128)S(1)} %log_add_fusion.2, pred[256,1024]{0,1:T(8,128)(4,1)S(1)} %compare_and_fusion.2, ...), kind=kOutput, calls=%fused_computation.8 | convolution fusion | flops 275251200 | bytes 7348224 | tf_op jit(solution)/shard_map/tgrd,ngd->grtn/dot_general | solution.py:34
  67.3 1.9 %fusion.142 = (f32[256,4]{0,1:T(4,128)S(1)}, bf16[256,1,4,128]{0,3,2,1:T(8,128)(2,1)}) fusion(bf16[256,1,4,128]{0,3,2,1:T(8,128)(2,1)S(1)} %bitcast.550, f32[1024,256,4]{1,0,2:T(8,128)S(1)} %get-tuple-element.167, f32[4,256]{1,0:T(4,128)S(1)} %log_add_fusion.1, pred[256,1024]{0,1:T(8,128)(4,1)S(1)} %compare_and_fusion.1, ...), kind=kOutput, calls=%fused_computation.127 | convolution fusion | flops 273808384 | bytes 5513216 | tf_op jit(solution)/shard_map/grtn,ngd->tgrd/dot_general | solution.py:29
  69.2 1.3 %fusion.3 = bf16[1,4,256,1024]{2,3,1,0:T(8,128)(2,1)S(1)} fusion(f32[1024,256,4]{1,0,2:T(8,128)S(1)} %get-tuple-element.167, bf16[256,4,128]{0,2,1:T(8,128)(2,1)S(1)} %bitcast.551, f32[4,256]{1,0:T(4,128)S(1)} %bitcast.561, f32[4,256]{1,0:T(4,128)S(1)} %log_add_fusion.1, pred[256,1024]{0,1:T(8,128)(4,1)S(1)} %compare_and_fusion.1, ...), kind=kOutput, calls=%fused_computation.5 | convolution fusion | flops 275251200 | bytes 7348224 | tf_op jit(solution)/shard_map/tgrd,ngd->grtn/dot_general | solution.py:34
  71.5 1.4 %fusion.49 = f32[2048,1,128]{0,2,1:T(8,128)S(1)} fusion(f32[2048,1,128]{0,2,1:T(8,128)S(1)} %scatter-add.25, bf16[256,4,128]{0,2,1:T(8,128)(2,1)S(1)} %bitcast.555, f32[1024,256,4]{1,0,2:T(8,128)S(1)} %get-tuple-element.169, f32[4,256]{1,0:T(4,128)S(1)} %log_add_fusion.2, pred[256,1024]{0,1:T(8,128)(4,1)S(1)} %compare_and_fusion.2), kind=kOutput, calls=%fused_computation.62 | convolution fusion | flops 272760832 | bytes 5771264 | tf_op jit(solution)/shard_map/grtn,tgrd->ngd/dot_general | solution.py:46
  72.9 1.4 %fusion.51 = f32[2048,1,128]{0,2,1:T(8,128)S(1)} fusion(f32[2048,1,128]{0,2,1:T(8,128)S(1)} %fusion.49, bf16[256,4,128]{0,2,1:T(8,128)(2,1)S(1)} %bitcast.552, f32[1024,256,4]{1,0,2:T(8,128)S(1)} %get-tuple-element.167, f32[4,256]{1,0:T(4,128)S(1)} %log_add_fusion.1, pred[256,1024]{0,1:T(8,128)(4,1)S(1)} %compare_and_fusion.1), kind=kOutput, calls=%fused_computation.64 | convolution fusion | flops 272760832 | bytes 5771264 | tf_op jit(solution)/shard_map/grtn,tgrd->ngd/dot_general | solution.py:46
  75.3 2.2 %collective-permute-start.1 = (bf16[1024,256]{0,1:T(8,128)(2,1)}, bf16[1024,256]{0,1:T(8,128)(2,1)}, u32[]{:S(2)}, u32[]{:S(2)}) collective-permute-start(bf16[1024,256]{0,1:T(8,128)(2,1)} %pad_maximum_fusion.3), channel_id=1, source_target_pairs={{8,0},{16,8},{24,16},{32,24},{40,32},{48,40},{56,48},{64,56},{72,6... | collective-permute-start | bytes 1572872 | tf_op jit(solution)/shard_map/ppermute | solution.py:14
  78.6 1.3 %copy.101 = bf16[1024,512]{1,0:T(8,128)(2,1)} copy(bf16[1024,512]{0,1:T(8,128)(2,1)S(1)} %bitcast.536) | data formatting | bytes 2097152
  81.2 1.3 %copy.100 = bf16[1024,512]{1,0:T(8,128)(2,1)} copy(bf16[1024,512]{0,1:T(8,128)(2,1)S(1)} %bitcast.537) | data formatting | bytes 2097152
  82.6 11.4 %collective-permute-done.1 = bf16[1024,256]{0,1:T(8,128)(2,1)} collective-permute-done((bf16[1024,256]{0,1:T(8,128)(2,1)}, bf16[1024,256]{0,1:T(8,128)(2,1)}, u32[]{:S(2)}, u32[]{:S(2)}) %collective-permute-start.1) | collective-permute-done | bytes 524320 | tf_op jit(solution)/shard_map/ppermute | solution.py:14
  95.1 3.6 %fusion.137 = bf16[1024,128]{0,1:T(8,128)(2,1)S(1)} fusion(f32[1024,256]{0,1:T(8,128)S(1)} %convert_element_type.219, bf16[256,4,128]{0,2,1:T(8,128)(2,1)S(1)} %bitcast.549, f32[2048,1,128]{0,2,1:T(8,128)} %copy-done.3, f32[1024,256,4]{1,0,2:T(8,128)} %copy-done.1, f32[4,256]{1,0:T(4,128)S(1)} %log_add_fusion, pred[256,1024]{0,1:T(8,128)(4,1)S(1)} %compare_and_fusion), kind=kOutput, calls=%fused_computation.118 | convolution fusion | flops 273022976 | bytes 6033408 | tf_op jit(solution)/shard_map/grtn,tgrd->ngd/dot_general | solution.py:46
  (90 shorter events, 32.0 us)
Async XLA Ops:
  0.6 1.4 %copy-start = (bf16[128,1024]{1,0:T(8,128)(2,1)S(1)}, bf16[128,1024]{1,0:T(8,128)(2,1)}, u32[]{:S(2)}) copy-start(bf16[128,1024]{1,0:T(8,128)(2,1)} %param.28) | copy-start | bytes 786436
  2.0 7.0 %copy-start.15 = (s32[128]{0:T(128)S(1)}, s32[128]{0:T(128)}, u32[]{:S(2)}) copy-start(s32[128]{0:T(128)} %param.31) | copy-start | bytes 1540
  2.0 7.3 %copy-start.4 = (bf16[1024,512]{1,0:T(8,128)(2,1)S(1)}, bf16[1024,512]{1,0:T(8,128)(2,1)}, u32[]{:S(2)}) copy-start(bf16[1024,512]{1,0:T(8,128)(2,1)} %param.30) | copy-start | bytes 3145732
  3.2 7.9 %copy-start.12 = (pred[1024]{0:T(1024)(128)(4,1)S(1)}, pred[1024]{0:T(1024)(128)(4,1)}, u32[]{:S(2)}) copy-start(pred[1024]{0:T(1024)(128)(4,1)} %constant.343) | copy-start | bytes 3076
  3.2 7.8 %copy-start.13 = (pred[1024]{0:T(1024)(128)(4,1)S(1)}, pred[1024]{0:T(1024)(128)(4,1)}, u32[]{:S(2)}) copy-start(pred[1024]{0:T(1024)(128)(4,1)} %constant.344) | copy-start | bytes 3076
  3.2 7.8 %copy-start.14 = (pred[1024]{0:T(1024)(128)(4,1)S(1)}, pred[1024]{0:T(1024)(128)(4,1)}, u32[]{:S(2)}) copy-start(pred[1024]{0:T(1024)(128)(4,1)} %constant.345) | copy-start | bytes 3076
  4.5 26.0 %all-to-all-start = ((bf16[128,8,768]{2,0,1:T(8,128)(2,1)}), bf16[128,8,768]{2,0,1:T(8,128)(2,1)S(1)}, u32[]{:S(2)}, u32[]{:S(2)}) async-start(bf16[128,8,768]{2,0,1:T(8,128)(2,1)} %pad_maximum_fusion), calls=%async_computation | async-start | bytes 3145728 | tf_op jit(solution)/shard_map/all_to_all | solution.py:65
  32.3 18.4 %collective-permute-start = (bf16[1024,256]{1,0:T(8,128)(2,1)}, bf16[1024,256]{1,0:T(8,128)(2,1)}, u32[]{:S(2)}, u32[]{:S(2)}) collective-permute-start(bf16[1024,256]{1,0:T(8,128)(2,1)} %slice.388), channel_id=1, source_target_pairs={{0,8},{8,16},{16,24},{24,32},{32,40},{40,48},{48,56},{56,64},{64,7... | collective-permute-start | bytes 1572872 | tf_op jit(solution)/shard_map/ppermute | solution.py:14
  38.5 1.7 %copy-start.7 = (bf16[256,512]{0,1:T(8,128)(2,1)S(1)}, bf16[256,512]{0,1:T(8,128)(2,1)}, u32[]{:S(2)}) copy-start(bf16[256,512]{0,1:T(8,128)(2,1)} %copy.146) | copy-start | bytes 786436
  39.3 2.9 %copy-start.1 = (f32[1024,256,4]{1,0,2:T(8,128)}, f32[1024,256,4]{1,0,2:T(8,128)S(1)}, u32[]{:S(2)}) copy-start(f32[1024,256,4]{1,0,2:T(8,128)S(1)} %get-tuple-element.165) | copy-start | bytes 12582916
  48.5 3.2 %copy-start.6 = (bf16[256,512]{0,1:T(8,128)(2,1)S(1)}, bf16[256,512]{0,1:T(8,128)(2,1)}, u32[]{:S(2)}) copy-start(bf16[256,512]{0,1:T(8,128)(2,1)} %copy.59) | copy-start | bytes 786436
  51.8 1.7 %copy-start.11 = (bf16[256,512]{0,1:T(8,128)(2,1)S(1)}, bf16[256,512]{0,1:T(8,128)(2,1)}, u32[]{:S(2)}) copy-start(bf16[256,512]{0,1:T(8,128)(2,1)} %copy.143) | copy-start | bytes 786436
  58.1 1.3 %copy-start.5 = (bf16[256,512]{0,1:T(8,128)(2,1)S(1)}, bf16[256,512]{0,1:T(8,128)(2,1)}, u32[]{:S(2)}) copy-start(bf16[256,512]{0,1:T(8,128)(2,1)} %copy.147) | copy-start | bytes 786436
  62.1 1.0 %copy-start.10 = (bf16[256,512]{0,1:T(8,128)(2,1)S(1)}, bf16[256,512]{0,1:T(8,128)(2,1)}, u32[]{:S(2)}) copy-start(bf16[256,512]{0,1:T(8,128)(2,1)} %copy.144) | copy-start | bytes 786436
  65.1 2.2 %copy-start.9 = (bf16[256,512]{0,1:T(8,128)(2,1)S(1)}, bf16[256,512]{0,1:T(8,128)(2,1)}, u32[]{:S(2)}) copy-start(bf16[256,512]{0,1:T(8,128)(2,1)} %copy.145) | copy-start | bytes 786436
  74.3 4.3 %copy-start.3 = (f32[2048,1,128]{0,2,1:T(8,128)}, f32[2048,1,128]{0,2,1:T(8,128)S(1)}, u32[]{:S(2)}) copy-start(f32[2048,1,128]{0,2,1:T(8,128)S(1)} %fusion.51) | copy-start | bytes 3145732
  75.3 18.6 %collective-permute-start.1 = (bf16[1024,256]{0,1:T(8,128)(2,1)}, bf16[1024,256]{0,1:T(8,128)(2,1)}, u32[]{:S(2)}, u32[]{:S(2)}) collective-permute-start(bf16[1024,256]{0,1:T(8,128)(2,1)} %pad_maximum_fusion.3), channel_id=1, source_target_pairs={{8,0},{16,8},{24,16},{32,24},{40,32},{48,40},{56,48},{64,56},{72,6... | collective-permute-start | bytes 1572872 | tf_op jit(solution)/shard_map/ppermute | solution.py:14
  78.6 16.5 %copy-start.8 = (bf16[256,512]{0,1:T(8,128)(2,1)S(1)}, bf16[256,512]{0,1:T(8,128)(2,1)}, u32[]{:S(2)}) copy-start(bf16[256,512]{0,1:T(8,128)(2,1)} %copy.146) | copy-start | bytes 786436
  82.6 16.1 %copy-start.2 = (bf16[1,4,256,1024]{2,3,1,0:T(8,128)(2,1)S(1)}, bf16[1,4,256,1024]{2,3,1,0:T(8,128)(2,1)}, u32[]{:S(2)}) copy-start(bf16[1,4,256,1024]{2,3,1,0:T(8,128)(2,1)} %fusion.1) | copy-start | bytes 6291460
where the time goes:
time: 102 us; the launch traced here: 101 us
  matrix products  32 us (31%)
  local copies, waits for them, and re-layouts  21.8 us (21%)
  waiting for transfers between devices  19.1 us (19%)
  other arithmetic  15.4 us (15%)
  starting transfers between devices  11.8 us (12%)
  between operations  1.19 us (1%)
    ppermute x2, waiting for transfers between devices, from_behind(): return lax.ppermute(block, axis, route)  11.4 us
    unnamed x40, local copies, waits for them, and re-layouts  9.71 us
    all_to_all x1, waiting for transfers between devices, local(): lax.all_to_all(packed, 'head', split_axis=1, concat_axis=0, tiled=True)  7.72 us
    dot_general x4, matrix products, tile_grads(): jnp.einsum('grtn,ngd->tgrd', weights_low, value_rows, preferred_element_t...  7.66 us
    dot_general x4, matrix products, tile_grads(): jnp.einsum('grtn,tgrd->ngd', weights_low, grad_tile, preferred_element_ty...  7.63 us
    ppermute x2, starting transfers between devices, from_behind(): return lax.ppermute(block, axis, route)  7.29 us
    dot_general x4, matrix products, tile_grads(): jnp.einsum('tgrd,ngd->grtn', grad_tile, value_rows, preferred_element_typ...  6.65 us
    gather x1, other arithmetic, local(): prior_doc = jnp.repeat(prior_units, unit_rows, total_repeat_length=ctx_rows)  5.04 us
  transfers between devices with their start and end apart: 3, of which 2 were waited for; matrix products, arithmetic and copies ran while one was open for 32% of the time, Pallas kernels for 0%

commit v1 on v0

--- a/solution.py
+++ b/solution.py
@@ -62,7 +62,15 @@
         ],
         axis=2,
     )
-    packed = lax.all_to_all(packed, "head", split_axis=1, concat_axis=0, tiled=True)
+    packed = jnp.concatenate(
+        jax.lax.all_to_all(
+            jnp.stack(jnp.split(packed, jax.lax.axis_size("head"), axis=1)),
+            axis_name="head",
+            split_axis=0,
+            concat_axis=0,
+        ),
+        axis=0,
+    )
     ctx_rows = packed.shape[0]
     packed = packed.reshape(ctx_rows, q_cols + 2 * k_cols)
     kv_local = k_cols // HEAD_SIZE

time: 102 us -> 102 us (level)
  other arithmetic: 15.4 us -> 14.1 us
  waiting for transfers between devices: 19.1 us -> 20.2 us
    unnamed x40 -> x48, local copies, waits for them, and re-layouts: 9.71 us -> 12.8 us
    reshape x2 -> x0, local copies, waits for them, and re-layouts: 2.52 us -> none  [the longest x1 1.36 us: local(): query_matrix.reshape(token_per_shard, head_groups, q_cols)]
    concatenate x1, other arithmetic: 1.29 us -> 0.11 us  [local(): jnp.concatenate([query_matrix.reshape(token_per_shard, head_groups, q_col...]
    all_to_all x1, waiting for transfers between devices: 7.72 us -> 8.85 us  [local(): jax.lax.all_to_all(jnp.stack(jnp.split(packed, jax.lax.axis_size('head'),...]
    another operation x4 -> x6, local copies, waits for them, and re-layouts: 3.12 us -> 4.04 us
  transfers between devices with their start and end apart: 3 -> 3, of which waited for: 2 -> 2; matrix products, arithmetic and copies ran while one was open for 32% -> 29% of each run, Pallas kernels for 0% -> 0%
where the time goes in v1:
time: 102 us
  matrix products  32 us (31%)
  local copies, waits for them, and re-layouts  22.2 us (22%)
  waiting for transfers between devices  20.2 us (20%)
  other arithmetic  14.1 us (14%)
  starting transfers between devices  11.8 us (12%)
  between operations  1.25 us (1%)
    unnamed x48, local copies, waits for them, and re-layouts  12.8 us
    ppermute x2, waiting for transfers between devices, from_behind(): return lax.ppermute(block, axis, route)  11.4 us
    all_to_all x1, waiting for transfers between devices, local(): jax.lax.all_to_all(jnp.stack(jnp.split(packed, jax.lax.axis_size('head'),...  8.85 us
    dot_general x4, matrix products, tile_grads(): jnp.einsum('grtn,ngd->tgrd', weights_low, value_rows, preferred_element_t...  7.66 us
    dot_general x4, matrix products, tile_grads(): jnp.einsum('grtn,tgrd->ngd', weights_low, grad_tile, preferred_element_ty...  7.63 us
    ppermute x2, starting transfers between devices, from_behind(): return lax.ppermute(block, axis, route)  7.29 us
    dot_general x4, matrix products, tile_grads(): jnp.einsum('tgrd,ngd->grtn', grad_tile, value_rows, preferred_element_typ...  6.66 us
    gather x1, other arithmetic, local(): prior_doc = jnp.repeat(prior_units, unit_rows, total_repeat_length=ctx_rows)  4.99 us
  transfers between devices with their start and end apart: 3, of which 2 were waited for; matrix products, arithmetic and copies ran while one was open for 29% of the time, Pallas kernels for 0%

profile of v1, /device:TPU:102, one launch (start us, length us, event | category | flops | bytes accessed | tf_op | source)
XLA Modules:
  0.0 101.5 jit_solution(8498487329621340668)
XLA Ops:
  0.6 1.6 %copy.164 = bf16[128,4096]{0,1:T(8,128)(2,1)S(1)} copy(bf16[128,4096]{1,0:T(8,128)(2,1)} %param.27) | data formatting | bytes 2097152 | tf_op args[0]
  5.0 1.6 %copy.167 = bf16[8,128,1,768]{3,1,2,0:T(8,128)(2,1)} copy(bf16[8,128,1,768]{1,3,2,0:T(8,128)(2,1)S(1)} %fusion.166) | data formatting | bytes 3145728 | tf_op jit(solution)/shard_map/stack | solution.py:67
  6.6 4.5 %all-to-all-start = ((bf16[8,128,1,768]{3,1,2,0:T(8,128)(2,1)}), bf16[8,128,1,768]{3,1,2,0:T(8,128)(2,1)S(1)}, u32[]{:S(2)}, u32[]{:S(2)}) async-start(bf16[8,128,1,768]{3,1,2,0:T(8,128)(2,1)} %copy.167), calls=%async_computation | async-start | bytes 3145728 | tf_op jit(solution)/shard_map/all_to_all | solution.py:66
  13.0 5.0 %select_select_fusion.1 = (s32[1024]{0:T(1024)S(1)}, s32[1024]{0:T(1024)S(1)}) fusion(pred[1024]{0:T(1024)(128)(4,1)S(1)} %copy-done.11, pred[1024]{0:T(1024)(128)(4,1)S(1)} %copy-done.12, pred[1024]{0:T(1024)(128)(4,1)S(1)} %copy-done.13, s32[]{:T(128)} %bitcast.20, s32[]{:T(128)} %bitcast.19, s32[]{:T(128)} %bitcast.18, s32[]{:T(128)} %bitcast.17, ...), kind=kLoop, calls=%fused_computation.184 | loop fusion | flops 6144 | bytes 11296 | tf_op jit(solution)/shard_map/jit(_take)/gather | solution.py:96
  18.0 1.8 %copy.253 = bf16[256,512]{0,1:T(8,128)(2,1)} copy(bf16[256,512]{1,0:T(8,128)(2,1)} %get-tuple-element.145) | data formatting | bytes 524288
  23.7 8.8 %all-to-all-done = bf16[8,128,1,768]{3,1,2,0:T(8,128)(2,1)S(1)} async-done(((bf16[8,128,1,768]{3,1,2,0:T(8,128)(2,1)}), bf16[8,128,1,768]{3,1,2,0:T(8,128)(2,1)S(1)}, u32[]{:S(2)}, u32[]{:S(2)}) %all-to-all-start) | async-done | bytes 1572896 | tf_op jit(solution)/shard_map/all_to_all | solution.py:66
  34.3 5.1 %collective-permute-start = (bf16[1024,256]{1,0:T(8,128)(2,1)}, bf16[1024,256]{1,0:T(8,128)(2,1)}, u32[]{:S(2)}, u32[]{:S(2)}) collective-permute-start(bf16[1024,256]{1,0:T(8,128)(2,1)} %slice.388), channel_id=1, source_target_pairs={{0,8},{8,16},{16,24},{24,32},{32,40},{40,48},{48,56},{56,64},{64,7... | collective-permute-start | bytes 1572872 | tf_op jit(solution)/shard_map/ppermute | solution.py:14
  42.2 1.9 %fusion.141 = (f32[256,4]{0,1:T(4,128)S(1)}, bf16[256,1,4,128]{0,3,2,1:T(8,128)(2,1)}) fusion(bf16[256,1,4,128]{0,3,2,1:T(8,128)(2,1)S(1)} %bitcast.565, f32[1024,256,4]{1,0,2:T(8,128)S(1)} %get-tuple-element.173, f32[4,256]{1,0:T(4,128)S(1)} %log_add_fusion, pred[256,1024]{0,1:T(8,128)(4,1)S(1)} %compare_and_fusion, bf16[1024,768]{1,0:T(8,128)(2,1)S(1)} %bitcast.548), kind=kOutput, calls=%fused_computation.124 | convolution fusion | flops 273284096 | bytes 5251072 | tf_op jit(solution)/shard_map/grtn,ngd->tgrd/dot_general | solution.py:29
  44.2 2.7 %fusion.1 = bf16[1,4,256,1024]{2,3,1,0:T(8,128)(2,1)} fusion(f32[1024,256,4]{1,0,2:T(8,128)S(1)} %get-tuple-element.173, bf16[256,4,128]{0,2,1:T(8,128)(2,1)S(1)} %bitcast.566, f32[4,256]{1,0:T(4,128)S(1)} %bitcast.580, f32[4,256]{1,0:T(4,128)S(1)} %log_add_fusion, pred[256,1024]{0,1:T(8,128)(4,1)S(1)} %compare_and_fusion, bf16[1024,768]{1,0:T(8,128)(2,1)S(1)} %bitcast.549), kind=kOutput, calls=%fused_computation.2 | convolution fusion | flops 274726912 | bytes 7086080 | tf_op jit(solution)/shard_map/tgrd,ngd->grtn/dot_general | solution.py:34
  48.9 2.1 %fusion.129 = bf16[256,1,4,128]{0,3,2,1:T(8,128)(2,1)S(1)} fusion(bf16[1,4,256,1024]{2,3,1,0:T(8,128)(2,1)} %fusion.1, bf16[1024,768]{1,0:T(8,128)(2,1)S(1)} %bitcast.550), kind=kOutput, calls=%fused_computation.96 | convolution fusion | flops 268697600 | bytes 2621440 | tf_op jit(solution)/shard_map/grtn,ngd->tgrd/dot_general | solution.py:39
  53.9 1.3 %convolution_bitcast_fusion.3 = f32[1024,1,128]{0,2,1:T(8,128)S(1)} fusion(bf16[256,4,128]{0,2,1:T(8,128)(2,1)S(1)} %bitcast.574, f32[1024,256,4]{1,0,2:T(8,128)S(1)} %get-tuple-element.179, f32[4,256]{1,0:T(4,128)S(1)} %log_add_fusion.3, pred[256,1024]{0,1:T(8,128)(4,1)S(1)} %fusion.136), kind=kOutput, calls=%fused_computation.60 | convolution fusion | flops 272629760 | bytes 5246976 | tf_op jit(solution)/shard_map/grtn,tgrd->ngd/dot_general | solution.py:46
  55.2 1.9 %fusion.144 = (f32[256,4]{0,1:T(4,128)S(1)}, bf16[256,1,4,128]{0,3,2,1:T(8,128)(2,1)}) fusion(bf16[256,1,4,128]{0,3,2,1:T(8,128)(2,1)S(1)} %bitcast.575, f32[1024,256,4]{1,0,2:T(8,128)S(1)} %get-tuple-element.179, f32[4,256]{1,0:T(4,128)S(1)} %log_add_fusion.3, pred[256,1024]{0,1:T(8,128)(4,1)S(1)} %fusion.136, ...), kind=kOutput, calls=%fused_computation.130 | convolution fusion | flops 273808384 | bytes 5513216 | tf_op jit(solution)/shard_map/grtn,ngd->tgrd/dot_general | solution.py:29
  57.1 1.3 %fusion.7 = bf16[1,4,256,1024]{2,3,1,0:T(8,128)(2,1)S(1)} fusion(f32[1024,256,4]{1,0,2:T(8,128)S(1)} %get-tuple-element.179, bf16[256,4,128]{0,2,1:T(8,128)(2,1)S(1)} %bitcast.576, f32[4,256]{1,0:T(4,128)S(1)} %bitcast.578, f32[4,256]{1,0:T(4,128)S(1)} %log_add_fusion.3, pred[256,1024]{0,1:T(8,128)(4,1)S(1)} %fusion.136, ...), kind=kOutput, calls=%fused_computation.11 | convolution fusion | flops 275251200 | bytes 7348224 | tf_op jit(solution)/shard_map/tgrd,ngd->grtn/dot_general | solution.py:34
  63.5 1.9 %fusion.143 = (f32[256,4]{0,1:T(4,128)S(1)}, bf16[256,1,4,128]{0,3,2,1:T(8,128)(2,1)}) fusion(bf16[256,1,4,128]{0,3,2,1:T(8,128)(2,1)S(1)} %bitcast.571, f32[1024,256,4]{1,0,2:T(8,128)S(1)} %get-tuple-element.177, f32[4,256]{1,0:T(4,128)S(1)} %log_add_fusion.2, pred[256,1024]{0,1:T(8,128)(4,1)S(1)} %compare_and_fusion.2, ...), kind=kOutput, calls=%fused_computation.128 | convolution fusion | flops 273808384 | bytes 5513216 | tf_op jit(solution)/shard_map/grtn,ngd->tgrd/dot_general | solution.py:29
  65.4 1.3 %fusion.5 = bf16[1,4,256,1024]{2,3,1,0:T(8,128)(2,1)S(1)} fusion(f32[1024,256,4]{1,0,2:T(8,128)S(1)} %get-tuple-element.177, bf16[256,4,128]{0,2,1:T(8,128)(2,1)S(1)} %bitcast.572, f32[4,256]{1,0:T(4,128)S(1)} %bitcast.581, f32[4,256]{1,0:T(4,128)S(1)} %log_add_fusion.2, pred[256,1024]{0,1:T(8,128)(4,1)S(1)} %compare_and_fusion.2, ...), kind=kOutput, calls=%fused_computation.8 | convolution fusion | flops 275251200 | bytes 7348224 | tf_op jit(solution)/shard_map/tgrd,ngd->grtn/dot_general | solution.py:34
  67.6 1.9 %fusion.142 = (f32[256,4]{0,1:T(4,128)S(1)}, bf16[256,1,4,128]{0,3,2,1:T(8,128)(2,1)}) fusion(bf16[256,1,4,128]{0,3,2,1:T(8,128)(2,1)S(1)} %bitcast.568, f32[1024,256,4]{1,0,2:T(8,128)S(1)} %get-tuple-element.175, f32[4,256]{1,0:T(4,128)S(1)} %log_add_fusion.1, pred[256,1024]{0,1:T(8,128)(4,1)S(1)} %compare_and_fusion.1, ...), kind=kOutput, calls=%fused_computation.126 | convolution fusion | flops 273808384 | bytes 5513216 | tf_op jit(solution)/shard_map/grtn,ngd->tgrd/dot_general | solution.py:29
  69.5 1.3 %fusion.3 = bf16[1,4,256,1024]{2,3,1,0:T(8,128)(2,1)S(1)} fusion(f32[1024,256,4]{1,0,2:T(8,128)S(1)} %get-tuple-element.175, bf16[256,4,128]{0,2,1:T(8,128)(2,1)S(1)} %bitcast.569, f32[4,256]{1,0:T(4,128)S(1)} %bitcast.579, f32[4,256]{1,0:T(4,128)S(1)} %log_add_fusion.1, pred[256,1024]{0,1:T(8,128)(4,1)S(1)} %compare_and_fusion.1, ...), kind=kOutput, calls=%fused_computation.5 | convolution fusion | flops 275251200 | bytes 7348224 | tf_op jit(solution)/shard_map/tgrd,ngd->grtn/dot_general | solution.py:34
  71.9 1.4 %fusion.49 = f32[2048,1,128]{0,2,1:T(8,128)S(1)} fusion(f32[2048,1,128]{0,2,1:T(8,128)S(1)} %scatter-add.25, bf16[256,4,128]{0,2,1:T(8,128)(2,1)S(1)} %bitcast.573, f32[1024,256,4]{1,0,2:T(8,128)S(1)} %get-tuple-element.177, f32[4,256]{1,0:T(4,128)S(1)} %log_add_fusion.2, pred[256,1024]{0,1:T(8,128)(4,1)S(1)} %compare_and_fusion.2), kind=kOutput, calls=%fused_computation.62 | convolution fusion | flops 272760832 | bytes 5771264 | tf_op jit(solution)/shard_map/grtn,tgrd->ngd/dot_general | solution.py:46
  73.3 1.4 %fusion.51 = f32[2048,1,128]{0,2,1:T(8,128)S(1)} fusion(f32[2048,1,128]{0,2,1:T(8,128)S(1)} %fusion.49, bf16[256,4,128]{0,2,1:T(8,128)(2,1)S(1)} %bitcast.570, f32[1024,256,4]{1,0,2:T(8,128)S(1)} %get-tuple-element.175, f32[4,256]{1,0:T(4,128)S(1)} %log_add_fusion.1, pred[256,1024]{0,1:T(8,128)(4,1)S(1)} %compare_and_fusion.1), kind=kOutput, calls=%fused_computation.64 | convolution fusion | flops 272760832 | bytes 5771264 | tf_op jit(solution)/shard_map/grtn,tgrd->ngd/dot_general | solution.py:46
  75.6 2.2 %collective-permute-start.1 = (bf16[1024,256]{0,1:T(8,128)(2,1)}, bf16[1024,256]{0,1:T(8,128)(2,1)}, u32[]{:S(2)}, u32[]{:S(2)}) collective-permute-start(bf16[1024,256]{0,1:T(8,128)(2,1)} %pad_maximum_fusion.3), channel_id=1, source_target_pairs={{8,0},{16,8},{24,16},{32,24},{40,32},{48,40},{56,48},{64,56},{72,6... | collective-permute-start | bytes 1572872 | tf_op jit(solution)/shard_map/ppermute | solution.py:14
  78.9 1.3 %copy.211 = bf16[1024,512]{1,0:T(8,128)(2,1)} copy(bf16[1024,512]{0,1:T(8,128)(2,1)S(1)} %bitcast.553) | data formatting | bytes 2097152
  81.5 1.3 %copy.210 = bf16[1024,512]{1,0:T(8,128)(2,1)} copy(bf16[1024,512]{0,1:T(8,128)(2,1)S(1)} %bitcast.554) | data formatting | bytes 2097152
  82.8 11.4 %collective-permute-done.1 = bf16[1024,256]{0,1:T(8,128)(2,1)} collective-permute-done((bf16[1024,256]{0,1:T(8,128)(2,1)}, bf16[1024,256]{0,1:T(8,128)(2,1)}, u32[]{:S(2)}, u32[]{:S(2)}) %collective-permute-start.1) | collective-permute-done | bytes 524320 | tf_op jit(solution)/shard_map/ppermute | solution.py:14
  95.4 3.6 %fusion.137 = bf16[1024,128]{0,1:T(8,128)(2,1)S(1)} fusion(f32[1024,256]{0,1:T(8,128)S(1)} %convert_element_type.219, bf16[256,4,128]{0,2,1:T(8,128)(2,1)S(1)} %bitcast.567, f32[2048,1,128]{0,2,1:T(8,128)} %copy-done.2, f32[1024,256,4]{1,0,2:T(8,128)} %copy-done, f32[4,256]{1,0:T(4,128)S(1)} %log_add_fusion, pred[256,1024]{0,1:T(8,128)(4,1)S(1)} %compare_and_fusion), kind=kOutput, calls=%fused_computation.117 | convolution fusion | flops 273022976 | bytes 6033408 | tf_op jit(solution)/shard_map/grtn,tgrd->ngd/dot_general | solution.py:46
  (98 shorter events, 31.6 us)
Async XLA Ops:
  4.7 6.3 %copy-start.14 = (s32[128]{0:T(128)S(1)}, s32[128]{0:T(128)}, u32[]{:S(2)}) copy-start(s32[128]{0:T(128)} %param.31) | copy-start | bytes 1540
  4.7 6.6 %copy-start.3 = (bf16[1024,512]{1,0:T(8,128)(2,1)S(1)}, bf16[1024,512]{1,0:T(8,128)(2,1)}, u32[]{:S(2)}) copy-start(bf16[1024,512]{1,0:T(8,128)(2,1)} %param.30) | copy-start | bytes 3145732
  4.9 8.0 %copy-start.11 = (pred[1024]{0:T(1024)(128)(4,1)S(1)}, pred[1024]{0:T(1024)(128)(4,1)}, u32[]{:S(2)}) copy-start(pred[1024]{0:T(1024)(128)(4,1)} %constant.343) | copy-start | bytes 3076
  4.9 8.0 %copy-start.12 = (pred[1024]{0:T(1024)(128)(4,1)S(1)}, pred[1024]{0:T(1024)(128)(4,1)}, u32[]{:S(2)}) copy-start(pred[1024]{0:T(1024)(128)(4,1)} %constant.344) | copy-start | bytes 3076
  5.0 8.0 %copy-start.13 = (pred[1024]{0:T(1024)(128)(4,1)S(1)}, pred[1024]{0:T(1024)(128)(4,1)}, u32[]{:S(2)}) copy-start(pred[1024]{0:T(1024)(128)(4,1)} %constant.345) | copy-start | bytes 3076
  6.6 26.0 %all-to-all-start = ((bf16[8,128,1,768]{3,1,2,0:T(8,128)(2,1)}), bf16[8,128,1,768]{3,1,2,0:T(8,128)(2,1)S(1)}, u32[]{:S(2)}, u32[]{:S(2)}) async-start(bf16[8,128,1,768]{3,1,2,0:T(8,128)(2,1)} %copy.167), calls=%async_computation | async-start | bytes 3145728 | tf_op jit(solution)/shard_map/all_to_all | solution.py:66
  34.3 16.8 %collective-permute-start = (bf16[1024,256]{1,0:T(8,128)(2,1)}, bf16[1024,256]{1,0:T(8,128)(2,1)}, u32[]{:S(2)}, u32[]{:S(2)}) collective-permute-start(bf16[1024,256]{1,0:T(8,128)(2,1)} %slice.388), channel_id=1, source_target_pairs={{0,8},{8,16},{16,24},{24,32},{32,40},{40,48},{48,56},{56,64},{64,7... | collective-permute-start | bytes 1572872 | tf_op jit(solution)/shard_map/ppermute | solution.py:14
  40.5 1.7 %copy-start.5 = (bf16[256,512]{0,1:T(8,128)(2,1)S(1)}, bf16[256,512]{0,1:T(8,128)(2,1)}, u32[]{:S(2)}) copy-start(bf16[256,512]{0,1:T(8,128)(2,1)} %copy.256) | copy-start | bytes 786436
  41.3 2.9 %copy-start = (f32[1024,256,4]{1,0,2:T(8,128)}, f32[1024,256,4]{1,0,2:T(8,128)S(1)}, u32[]{:S(2)}) copy-start(f32[1024,256,4]{1,0,2:T(8,128)S(1)} %get-tuple-element.173) | copy-start | bytes 12582916
  48.9 3.2 %copy-start.4 = (bf16[256,512]{0,1:T(8,128)(2,1)S(1)}, bf16[256,512]{0,1:T(8,128)(2,1)}, u32[]{:S(2)}) copy-start(bf16[256,512]{0,1:T(8,128)(2,1)} %copy.169) | copy-start | bytes 786436
  52.1 1.7 %copy-start.9 = (bf16[256,512]{0,1:T(8,128)(2,1)S(1)}, bf16[256,512]{0,1:T(8,128)(2,1)}, u32[]{:S(2)}) copy-start(bf16[256,512]{0,1:T(8,128)(2,1)} %copy.253) | copy-start | bytes 786436
  62.5 1.0 %copy-start.8 = (bf16[256,512]{0,1:T(8,128)(2,1)S(1)}, bf16[256,512]{0,1:T(8,128)(2,1)}, u32[]{:S(2)}) copy-start(bf16[256,512]{0,1:T(8,128)(2,1)} %copy.254) | copy-start | bytes 786436
  65.4 2.2 %copy-start.7 = (bf16[256,512]{0,1:T(8,128)(2,1)S(1)}, bf16[256,512]{0,1:T(8,128)(2,1)}, u32[]{:S(2)}) copy-start(bf16[256,512]{0,1:T(8,128)(2,1)} %copy.255) | copy-start | bytes 786436
  74.6 4.3 %copy-start.2 = (f32[2048,1,128]{0,2,1:T(8,128)}, f32[2048,1,128]{0,2,1:T(8,128)S(1)}, u32[]{:S(2)}) copy-start(f32[2048,1,128]{0,2,1:T(8,128)S(1)} %fusion.51) | copy-start | bytes 3145732
  75.6 18.6 %collective-permute-start.1 = (bf16[1024,256]{0,1:T(8,128)(2,1)}, bf16[1024,256]{0,1:T(8,128)(2,1)}, u32[]{:S(2)}, u32[]{:S(2)}) collective-permute-start(bf16[1024,256]{0,1:T(8,128)(2,1)} %pad_maximum_fusion.3), channel_id=1, source_target_pairs={{8,0},{16,8},{24,16},{32,24},{40,32},{48,40},{56,48},{64,56},{72,6... | collective-permute-start | bytes 1572872 | tf_op jit(solution)/shard_map/ppermute | solution.py:14
  78.3 2.0 %copy-start.10 = (bf16[256,1,4,128]{0,3,2,1:T(8,128)(2,1)S(1)}, bf16[256,1,4,128]{0,3,2,1:T(8,128)(2,1)}, u32[]{:S(2)}) copy-start(bf16[256,1,4,128]{0,3,2,1:T(8,128)(2,1)} %get-tuple-element.181) | copy-start | bytes 786436
  78.9 16.5 %copy-start.6 = (bf16[256,512]{0,1:T(8,128)(2,1)S(1)}, bf16[256,512]{0,1:T(8,128)(2,1)}, u32[]{:S(2)}) copy-start(bf16[256,512]{0,1:T(8,128)(2,1)} %copy.256) | copy-start | bytes 786436
  82.8 16.2 %copy-start.1 = (bf16[1,4,256,1024]{2,3,1,0:T(8,128)(2,1)S(1)}, bf16[1,4,256,1024]{2,3,1,0:T(8,128)(2,1)}, u32[]{:S(2)}) copy-start(bf16[1,4,256,1024]{2,3,1,0:T(8,128)(2,1)} %fusion.1) | copy-start | bytes 6291460
